TPU v7x, 256 devices: a whole 4x4x8 slice. The times are simulated.
256 devices in a mesh: ctx: 32 (over x, z), head: 8 (over y, core).
Axes of the slice: x: 4, y: 4, z: 8, core: 2. Of those that a mesh axis runs over, the one named last changes fastest.
Arguments:
- features: bfloat16 [8192, 16384], P('ctx', 'head'), may hold values from -6 to 6
- log_decay: float32 [256, 8192], P('head', 'ctx'), may hold values from -2 to 0, as said below
- step_size: float32 [256, 8192], P('head', 'ctx'), may hold values from 0.0002 to 0.002
- b_matrix: bfloat16 [8192, 2048], P('ctx', 'head'), may hold values from -6 to 6
- c_matrix: bfloat16 [8192, 2048], P('ctx', 'head'), may hold values from -6 to 6
- skip_gain: float32 [256], P('head'), may hold values from 0.5 to 1.5
Outputs:
- mixed: bfloat16 [8192, 16384], P('ctx', 'head')
Inputs may be any that keep to these rules, and one draw needn't show every extreme that they name: `log_decay`: every entry is negative.
All inputs are finite; a program needn't handle non-finite values.
Results may differ from a plain program's by a relative error of at most 0.0013.
Values sent between devices are 32-bit elements; how exact they have to be, the bound alone decides.
No kernel may reach another device: no remote copies, remote signals or barrier semaphores. Data moves between devices by JAX's collectives and lax.ppermute only.
A program may use at most 320 MiB of HBM per device.

v0:
```python
import jax
import jax.numpy as jnp
from jax import lax
from jax.sharding import PartitionSpec as P

N = 256
SPAN = 128


def carried_in(x, axis, combine, identity, reverse):
    length, place = (lax.axis_size(axis), lax.axis_index(axis))
    everything = jax.tree.map(lambda part: lax.all_gather(part, axis), x)
    start = jax.tree.map(
        lambda part, zero: jnp.broadcast_to(jnp.asarray(zero, part.dtype), part.shape), x, identity
    )

    def step(k, before):
        at = length - 1 - k if reverse else k
        reached = at > place if reverse else at < place
        new = combine(before, jax.tree.map(lambda part: part[at], everything))
        return jax.tree.map(lambda a, b: jnp.where(reached, a, b), new, before)

    return lax.fori_loop(0, length, step, start)


def from_root(block, axis, source):
    block = jnp.where(lax.axis_index(axis) == source, block, jnp.zeros_like(block))
    return lax.psum(block, axis)


def chain(earlier, later_pair):
    return (
        earlier[0] + later_pair[0],
        jnp.exp(later_pair[0])[:, None, None] * earlier[1] + later_pair[1],
    )


def on_device(features, log_decay, step_size, b_matrix, c_matrix, skip_gain):
    head_count = log_decay.shape[0]
    tok_rows = features.shape[0]
    head_width = features.shape[1] // head_count
    state_size = N
    group_count = b_matrix.shape[1] // state_size
    per_group = head_count // group_count
    span_count = tok_rows // SPAN
    half_count = span_count // 2
    cumulative = jnp.cumsum(log_decay.reshape(head_count, span_count, SPAN), axis=2)
    step_rows = step_size.reshape(head_count, span_count, SPAN)
    inputs = features.reshape(span_count, SPAN, head_count, head_width)
    grouped_inputs = features.reshape(span_count, SPAN, group_count, per_group, head_width)
    b_spans = b_matrix.reshape(span_count, SPAN, group_count, state_size)
    c_spans = c_matrix.reshape(span_count, SPAN, group_count, state_size)
    scores = jnp.einsum("ktgn,ksgn->gkts", c_spans, b_spans, preferred_element_type=jnp.float32)
    causal = jnp.arange(SPAN)[:, None] >= jnp.arange(SPAN)[None, :]
    cum_grouped = cumulative.reshape(group_count, per_group, span_count, SPAN)
    step_grouped = step_rows.reshape(group_count, per_group, span_count, SPAN)
    decay_gaps = jnp.where(causal, cum_grouped[..., :, None] - cum_grouped[..., None, :], -jnp.inf)
    weights = (scores[:, None] * jnp.exp(decay_gaps) * step_grouped[:, :, :, None, :]).astype(
        jnp.bfloat16
    )
    diagonal_part = jnp.einsum(
        "gqkts,ksgqp->ktgqp", weights, grouped_inputs, preferred_element_type=jnp.float32
    )
    diagonal_part = diagonal_part.reshape(span_count, SPAN, head_count, head_width)
    span_ends = cumulative[:, :, -1]
    coeffs = jnp.exp(span_ends[:, :, None] - cumulative) * step_rows
    weighted = (inputs * jnp.transpose(coeffs, (1, 2, 0))[:, :, :, None]).astype(jnp.bfloat16)
    weighted = weighted.reshape(span_count, SPAN, group_count, per_group, head_width)
    span_states = jnp.einsum(
        "ksgn,ksgqp->kgqpn", b_spans, weighted, preferred_element_type=jnp.float32
    )
    span_states = span_states.reshape(span_count, head_count, head_width, state_size)
    totals = jnp.transpose(span_ends).reshape(2, half_count, head_count)
    grouped = span_states.reshape(2, half_count, head_count, head_width, state_size)

    def advance(running, element):
        return (jnp.exp(element[0])[:, :, None, None] * running + element[1], running)

    start = jnp.zeros((2, head_count, head_width, state_size), jnp.float32)
    block_states, prefix = lax.scan(
        advance, start, (jnp.swapaxes(totals, 0, 1), jnp.swapaxes(grouped, 0, 1))
    )
    shifted = jnp.concatenate([jnp.zeros((2, 1, head_count), jnp.float32), totals[:, :-1]], axis=1)
    before = jnp.cumsum(shifted, axis=1)
    block_decay = jnp.sum(totals, axis=1)
    front_pair = (block_decay[0], block_states[0])
    back_pair = (block_decay[1], block_states[1])
    neutral = (
        jnp.zeros((head_count,), jnp.float32),
        jnp.zeros((head_count, head_width, state_size), jnp.float32),
    )
    enter_front = carried_in(front_pair, "ctx", chain, neutral, False)
    through_front = chain(enter_front, front_pair)[1]
    middle = from_root(through_front, "ctx", lax.axis_size("ctx") - 1)
    behind = carried_in(back_pair, "ctx", chain, neutral, True)
    enter_back = jnp.exp(behind[0])[:, None, None] * middle + behind[1]
    entering = jnp.stack([enter_front[1], enter_back])
    span_enter = jnp.exp(before)[:, :, :, None, None] * entering[:, None] + jnp.swapaxes(
        prefix, 0, 1
    )
    state_bf = span_enter.astype(jnp.bfloat16)
    state_part = jnp.einsum(
        "ktgn,kgqpn->ktgqp", c_spans, state_bf, preferred_element_type=jnp.float32
    )
    state_part = state_part.reshape(span_count, SPAN, head_count, head_width)
    state_part = state_part * jnp.transpose(jnp.exp(cumulative), (1, 2, 0))[:, :, :, None]
    output_rows = (
        diagonal_part + state_part + skip_gain[None, None, :, None] * inputs.astype(jnp.float32)
    )
    return output_rows.reshape(tok_rows, head_count * head_width).astype(jnp.bfloat16)


def solution(mesh):
    placed = (
        P("ctx", "head"),
        P("head", "ctx"),
        P("head", "ctx"),
        P("ctx", "head"),
        P("ctx", "head"),
        P("head"),
    )
    return jax.shard_map(
        on_device, mesh=mesh, in_specs=placed, out_specs=P("ctx", "head"), check_vma=False
    )
```

profile of v0, /device:TPU:8, one launch (start us, length us, event | category | flops | bytes accessed | tf_op | source)
XLA Modules:
  0.0 1049.9 jit_solution(3869095595849692370)
XLA Ops:
  23.7 43.5 %all-gather = f32[32,1,32]{2,1,0:T(1,128)S(1)} all-gather(f32[1,1,32]{2,1,0:T(1,128)S(1)} %get-tuple-element.343), channel_id=1, replica_groups=mesh['ctx'=32,'head'=8] {'ctx'}, dimensions={0}, use_global_device_ids=true | all-gather | bytes 4224 | tf_op jit(solution)/shard_map/all_gather | solution.py:12
  67.2 38.4 %all-gather.1 = f32[32,1,32]{2,1,0:T(1,128)S(1)} all-gather(f32[1,1,32]{2,1,0:T(1,128)S(1)} %get-tuple-element.342), channel_id=1, replica_groups=mesh['ctx'=32,'head'=8] {'ctx'}, dimensions={0}, use_global_device_ids=true | all-gather | bytes 4224 | tf_op jit(solution)/shard_map/all_gather | solution.py:12
  105.6 344.3 %all-gather.5.cloned.1.call-done = f32[32,32,64,256]{3,2,1,0:T(8,128)} async-done(((f32[1,32,64,256]{3,2,1,0:T(8,128)}), f32[32,32,64,256]{3,2,1,0:T(8,128)}) %all-gather.5.cloned.1.call-update) | async-done | bytes 67108880 | tf_op jit(solution)/shard_map/all_gather | solution.py:12
  449.9 127.7 %while.37 = (s32[]{:T(128)}, f32[32,64,256]{2,1,0:T(8,128)}, s32[]{:T(128)}, f32[32,32]{1,0:T(8,128)S(1)}, f32[32,32,64,256]{3,2,1,0:T(8,128)}, /*index=5*/s32[]{:T(128)}, s32[]{:T(128)}) while((s32[]{:T(128)}, f32[32,64,256]{2,1,0:T(8,128)}, s32[]{:T(128)}, f32[32,32]{1,0:T(8,128)S(1)}, f32[32,32,64,256]{3,2,1,0:T(8,128)}, ...), condition=%wide.region_2.3_spmd.clone, body=%wide.region_1.2_spmd.clone.sunk | while | flops 2097156 | bytes 6291945 | solution.py:23
  457.1 3.9 fusion.37
  461.0 4.6 fusion.37
  465.6 4.3 fusion.37
  473.8 3.9 fusion.37
  477.8 4.0 fusion.37
  481.7 3.9 fusion.37
  485.7 3.9 fusion.37
  489.6 3.9 fusion.37
  493.5 3.9 fusion.37
  497.4 4.0 fusion.37
  501.4 3.9 fusion.37
  505.4 3.9 fusion.37
  509.3 3.9 fusion.37
  513.2 3.9 fusion.37
  517.1 4.0 fusion.37
  521.1 3.9 fusion.37
  525.0 3.9 fusion.37
  528.9 3.9 fusion.37
  532.9 3.9 fusion.37
  536.7 3.9 fusion.37
  556.2 4.1 fusion.37
  560.3 5.1 fusion.37
  565.5 4.3 fusion.37
  573.6 4.0 fusion.37
  577.6 4.9 convert_bitcast_fusion
  582.5 298.2 %all-gather.7.cloned.1.call-done = f32[32,32,64,256]{3,2,1,0:T(8,128)} async-done(((f32[1,32,64,256]{3,2,1,0:T(8,128)}), f32[32,32,64,256]{3,2,1,0:T(8,128)}) %all-gather.7.cloned.1.call-update) | async-done | bytes 67108880 | tf_op jit(solution)/shard_map/all_gather | solution.py:12
  880.7 69.6 %while.38 = (s32[]{:T(128)}, f32[32]{0:T(128)S(1)}, f32[32,64,256]{2,1,0:T(8,128)S(1)}, s32[]{:T(128)}, f32[32,32]{1,0:T(8,128)S(1)}, /*index=5*/f32[32,32,64,25...) while((s32[]{:T(128)}, f32[32]{0:T(128)S(1)}, f32[32,64,256]{2,1,0:T(8,128)S(1)}, ...), condition=%wide.region_4.5_spmd.clone, body=%wide.region_3.4_spmd.clone.sunk | while | flops 2097256 | bytes 6292273 | solution.py:23
  950.3 85.2 %all-reduce.2.cloned.1.call-done = f32[32,64,256]{2,1,0:T(8,128)} async-done(((f32[32,64,256]{2,1,0:T(8,128)}), f32[32,64,256]{2,1,0:T(8,128)}) %all-reduce.2.cloned.1.call-update) | async-done | bytes 2097168 | tf_op jit(solution)/shard_map/psum | solution.py:28
  (156 shorter events, 124.0 us)
Async XLA Ops:
  6.5 5.3 copy-start
  6.5 443.4 %all-gather.5.cloned.1.call-start = ((), (), s32[]{:S(2)}) async-start(), calls=%async_computation | async-start | bytes 69206016 | tf_op jit(solution)/shard_map/all_gather | solution.py:12
  10.8 1.8 copy-start.3
  12.6 3.3 copy-start.1
  15.8 0.9 copy-start.6
  15.8 0.9 copy-start.5
  15.9 864.8 %all-gather.7.cloned.1.call-start = ((), (), s32[]{:S(2)}) async-start(), calls=%async_computation.1 | async-start | bytes 69206016 | tf_op jit(solution)/shard_map/all_gather | solution.py:12
  16.6 1018.8 %all-reduce.2.cloned.1.call-start = ((), (), s32[]{:S(2)}) async-start(), calls=%async_computation.2 | async-start | bytes 4194304 | tf_op jit(solution)/shard_map/psum | solution.py:28
  20.6 3.0 copy-start.7
  1035.5 2.0 copy-start.4
  1039.8 1.6 copy-start.2
Sparse Core Ops, SparseCore 0:
  16.0 433.8 all-gather.4
  452.5 428.1 all-gather.6
  884.2 151.2 all-reduce.1
where the time goes:
time: 1050 us
  waiting for transfers between devices  728 us (69%)
  other arithmetic  206 us (20%)
  blocking collectives  81.9 us (8%)
  local copies, waits for them, and re-layouts  14.1 us (1%)
  between operations  13.3 us (1%)
    all_gather x2, waiting for transfers between devices, carried_in(): everything = jax.tree.map(lambda part: lax.all_gather(part, axis), x)  642 us
    select_n x64, other arithmetic, step(): return jax.tree.map(lambda a, b: jnp.where(reached, a, b), new, before)  195 us
    psum x1, waiting for transfers between devices, from_root(): return lax.psum(block, axis)  85.2 us
    all_gather x2, blocking collectives, carried_in(): everything = jax.tree.map(lambda part: lax.all_gather(part, axis), x)  81.9 us
  transfers between devices with their start and end apart: 3, of which 3 were waited for; matrix products, arithmetic and copies ran while one was open for 20% of the time, Pallas kernels for 0%

commit v1 on v0

--- a/solution.py
+++ b/solution.py
@@ -5,6 +5,10 @@
 
 N = 256
 SPAN = 128
+
+
+def show_case(u, dev_axis):
+    return lax.all_gather(u, axis_name=dev_axis).sum(axis=0)
 
 
 def carried_in(x, axis, combine, identity, reverse):
@@ -25,7 +29,7 @@
 
 def from_root(block, axis, source):
     block = jnp.where(lax.axis_index(axis) == source, block, jnp.zeros_like(block))
-    return lax.psum(block, axis)
+    return show_case(block, axis)
 
 
 def chain(earlier, later_pair):

time: 1050 us -> 1350 us (1.29)
  waiting for transfers between devices: 728 us -> 1060 us
  other arithmetic: 206 us -> 170 us
    all_gather x0 -> x1, waiting for transfers between devices: none -> 360 us  [show_case(): return lax.all_gather(u, axis_name=dev_axis).sum(axis=0)]
    psum x1 -> x0, waiting for transfers between devices: 85.2 us -> none  [from_root(): return lax.psum(block, axis)]
    all_gather x2, waiting for transfers between devices: 642 us -> 701 us  [carried_in(): everything = jax.tree.map(lambda part: lax.all_gather(part, axis), x)]
    select_n x64, other arithmetic: 195 us -> 138 us  [step(): return jax.tree.map(lambda a, b: jnp.where(reached, a, b), new, before)]
    reduce_sum x0 -> x1, other arithmetic: none -> 22.2 us  [show_case(): return lax.all_gather(u, axis_name=dev_axis).sum(axis=0)]
  transfers between devices with their start and end apart: 3 -> 3, of which waited for: 3 -> 3; matrix products, arithmetic and copies ran while one was open for 20% -> 11% of each run, Pallas kernels for 0% -> 0%
where the time goes in v1:
time: 1350 us
  waiting for transfers between devices  1060 us (79%)
  other arithmetic  170 us (13%)
  blocking collectives  81.1 us (6%)
  local copies, waits for them, and re-layouts  15 us (1%)
    all_gather x2, waiting for transfers between devices, carried_in(): everything = jax.tree.map(lambda part: lax.all_gather(part, axis), x)  701 us
    all_gather x1, waiting for transfers between devices, show_case(): return lax.all_gather(u, axis_name=dev_axis).sum(axis=0)  360 us
    select_n x64, other arithmetic, step(): return jax.tree.map(lambda a, b: jnp.where(reached, a, b), new, before)  138 us
    all_gather x2, blocking collectives, carried_in(): everything = jax.tree.map(lambda part: lax.all_gather(part, axis), x)  81.1 us
  transfers between devices with their start and end apart: 3, of which 3 were waited for; matrix products, arithmetic and copies ran while one was open for 11% of the time, Pallas kernels for 0%

profile of v1, /device:TPU:8, one launch (start us, length us, event | category | flops | bytes accessed | tf_op | source)
XLA Modules:
  0.0 1348.0 jit_solution(5261642748415804444)
XLA Ops:
  12.6 2.5 fusion.26
  16.6 43.0 %all-gather.1 = f32[32,1,32]{2,1,0:T(1,128)S(1)} all-gather(f32[1,1,32]{2,1,0:T(1,128)S(1)} %get-tuple-element.343), channel_id=1, replica_groups=mesh['ctx'=32,'head'=8] {'ctx'}, dimensions={0}, use_global_device_ids=true | all-gather | bytes 4224 | tf_op jit(solution)/shard_map/all_gather | solution.py:16
  59.6 390.3 %all-gather.7.cloned.1.call-done = f32[32,32,64,256]{3,2,1,0:T(8,128)} async-done(((f32[1,32,64,256]{3,2,1,0:T(8,128)}), f32[32,32,64,256]{3,2,1,0:T(8,128)}) %all-gather.7.cloned.1.call-update) | async-done | bytes 67108880 | tf_op jit(solution)/shard_map/all_gather | solution.py:16
  449.9 70.4 %while.37 = (s32[]{:T(128)}, f32[32,64,256]{2,1,0:T(8,128)S(1)}, s32[]{:T(128)}, f32[32,32]{1,0:T(8,128)S(1)}, f32[32,32,64,256]{3,2,1,0:T(8,128)}, /*index=5*/s32[]{:T(128)}, s32[]{:T(128)}) while((s32[]{:T(128)}, f32[32,64,256]{2,1,0:T(8,128)S(1)}, s32[]{:T(128)}, f32[32,32]{1,0:T(8,128)S(1)}, f32[32,32,64,256]{3,2,1,0:T(8,128)}, ...), condition=%wide.region_2.3_spmd.clone, body=%wide.region_1.2_spmd.clone.sunk | while | flops 2097156 | bytes 6291945 | solution.py:27
  460.6 2.5 fusion.37
  463.1 2.4 fusion.37
  465.6 2.5 fusion.37
  472.4 2.2 fusion.37
  474.6 2.2 fusion.37
  492.0 2.2 fusion.37
  498.6 2.2 fusion.37
  500.8 2.2 fusion.37
  520.3 3.7 convert_bitcast_fusion
  525.1 3.6 fusion.20
  528.7 3.0 copy.27
  531.9 38.1 %all-gather.2 = f32[32,1,32]{2,1,0:T(1,128)S(1)} all-gather(f32[1,1,32]{2,1,0:T(1,128)S(1)} %get-tuple-element.342), channel_id=1, replica_groups=mesh['ctx'=32,'head'=8] {'ctx'}, dimensions={0}, use_global_device_ids=true | all-gather | bytes 4224 | tf_op jit(solution)/shard_map/all_gather | solution.py:16
  570.0 310.7 %all-gather.9.cloned.1.call-done = f32[32,32,64,256]{3,2,1,0:T(8,128)} async-done(((f32[1,32,64,256]{3,2,1,0:T(8,128)}), f32[32,32,64,256]{3,2,1,0:T(8,128)}) %all-gather.9.cloned.1.call-update) | async-done | bytes 67108880 | tf_op jit(solution)/shard_map/all_gather | solution.py:16
  880.6 70.8 %while.38 = (s32[]{:T(128)}, f32[32]{0:T(128)S(1)}, f32[32,64,256]{2,1,0:T(8,128)S(1)}, s32[]{:T(128)}, f32[32,32]{1,0:T(8,128)S(1)}, /*index=5*/f32[32,32,64,25...) while((s32[]{:T(128)}, f32[32]{0:T(128)S(1)}, f32[32,64,256]{2,1,0:T(8,128)S(1)}, ...), condition=%wide.region_4.5_spmd.clone, body=%wide.region_3.4_spmd.clone.sunk | while | flops 2097256 | bytes 6292273 | solution.py:27
  891.4 2.5 fusion.38
  893.9 2.4 fusion.38
  896.4 2.5 fusion.38
  903.3 2.2 fusion.38
  905.5 2.2 fusion.38
  907.7 2.1 fusion.38
  912.1 2.1 fusion.38
  914.3 2.1 fusion.38
  923.0 2.2 fusion.38
  925.2 2.2 fusion.38
  931.8 2.2 fusion.38
  934.0 2.1 fusion.38
  951.4 359.9 %all-gather.11.cloned.1.call-done = f32[1024,64,256]{2,1,0:T(8,128)} async-done(((f32[32,64,256]{2,1,0:T(8,128)}), f32[1024,64,256]{2,1,0:T(8,128)}) %all-gather.11.cloned.1.call-update) | async-done | bytes 67108880 | tf_op jit(solution)/shard_map/all_gather | solution.py:11
  1311.4 22.2 %reduce_sum.8 = f32[32,64,256]{2,1,0:T(8,128)} reduce(f32[32,32,64,256]{3,2,1,0:T(8,128)} %bitcast.16, f32[]{:T(128)} %constant.95.clone.1), dimensions={0}, to_apply=%region_5.6 | reduce | flops 16252928 | bytes 69206016 | tf_op jit(solution)/shard_map/reduce_sum | solution.py:11
  (157 shorter events, 110.7 us)
Async XLA Ops:
  6.5 5.3 copy-start
  6.5 443.3 %all-gather.7.cloned.1.call-start = ((), (), s32[]{:S(2)}) async-start(), calls=%async_computation | async-start | bytes 69206016 | tf_op jit(solution)/shard_map/all_gather | solution.py:16
  10.8 1.8 copy-start.3
  12.6 3.2 copy-start.1
  15.8 864.8 %all-gather.9.cloned.1.call-start = ((), (), s32[]{:S(2)}) async-start(), calls=%async_computation.1 | async-start | bytes 69206016 | tf_op jit(solution)/shard_map/all_gather | solution.py:16
  16.6 1294.8 %all-gather.11.cloned.1.call-start = ((), (), s32[]{:S(2)}) async-start(), calls=%async_computation.2 | async-start | bytes 69206016 | tf_op jit(solution)/shard_map/all_gather | solution.py:11
  524.0 0.8 copy-start.6
  524.0 0.9 copy-start.5
  528.7 3.0 copy-start.7
  1333.5 2.0 copy-start.4
  1337.9 1.6 copy-start.2
Sparse Core Ops, SparseCore 0:
  15.9 433.8 all-gather.6
  452.5 428.1 all-gather.8
  883.2 428.1 all-gather.10
